TPU v7x, 256 devices: a whole 4x4x8 slice. The times are simulated.
256 devices in a mesh: row: 16 (over y_hi, x, core), col: 16 (over z, y_lo).
Axes of the slice: x: 4, y: 4 (y_hi: 2, y_lo: 2; y = y_hi * 2 + y_lo), z: 8, core: 2. Of those that a mesh axis runs over, the one named last changes fastest.
Arguments:
- inputs: bfloat16 [1024, 16384], P('col', 'row'), may hold values from -6 to 6
- out_grad: bfloat16 [1024, 16384], P('col', 'row'), may hold values from -0.1875 to 0.1875
- states: bfloat16 [16384, 1024], P(('col', 'row')), may hold values from -6 to 6
- in_weight: bfloat16 [16384, 16384], P('row', 'col'), may hold values from -0.046875 to 0.046875
- out_weight: bfloat16 [16384, 16384], P('col', 'row'), may hold values from -0.046875 to 0.046875
- decay_rate: float32 [4, 16384], P(None, ('col', 'row')), may hold values from 0.0015625 to 0.1
- session_ids: int32 [4], replicated, may hold values from 0 to 3, each once
- lengths: int32 [4], replicated, may hold values from 1 to 256, 640 in all
Outputs:
- input_grad: bfloat16 [1024, 16384], P('col', 'row')
- in_weight_grad: bfloat16 [16384, 16384], P('row', 'col')
- out_weight_grad: bfloat16 [16384, 16384], P('col', 'row')
- rate_grad: float32 [4, 16384], P(None, ('col', 'row'))
Inputs may be any that keep to these rules, and one draw needn't show every extreme that they name: `session_ids`: each session appears in exactly one sequence. The lengths sum to 640.
All inputs are finite; a program needn't handle non-finite values.
Results may differ from a plain program's by a relative error of at most 0.024.
Values may be sent and summed in bfloat16 or wider, within the bound.
No kernel may reach another device: no remote copies, remote signals or barrier semaphores. Data moves between devices by JAX's collectives and lax.ppermute only.
A program may use at most 128 MiB of HBM per device.

v0:
```python
import jax
import jax.numpy as jnp
from jax import lax
from jax.sharding import PartitionSpec as P

exact_mode = lax.Precision.HIGHEST


def contract(left_side, right_side, left_dim, right_dim):
    return lax.dot_general(
        left_side,
        right_side,
        (((left_dim,), (right_dim,)), ((), ())),
        preferred_element_type=jnp.float32,
    )


def session_table(session_ids, table_rows):
    return (session_ids[:, None] == jnp.arange(table_rows, dtype=jnp.int32)[None, :]).astype(
        jnp.float32
    )


def gather_rows(share, axis_name, parts):
    spread = jnp.broadcast_to(share[None], (parts,) + share.shape)
    return lax.all_to_all(spread, axis_name, 0, 0).reshape((-1,) + share.shape[1:])


def scatter_sum(partial, axis_name, parts):
    pieces = lax.all_to_all(partial.reshape((parts, -1) + partial.shape[1:]), axis_name, 0, 0)
    return jnp.sum(pieces.astype(jnp.float32), axis=0)


def adjoint_sweep(state_grad, rate_rows, onehot, seq_count):
    channels = state_grad.shape[0]
    seq_rate = jnp.dot(onehot, rate_rows, precision=exact_mode)
    decays = (1.0 - seq_rate).T
    running = state_grad.reshape(channels, seq_count, -1)
    bins = running.shape[2]
    factor = decays[:, :, None]
    shift = 1
    while shift < bins:
        ahead = jnp.concatenate(
            [running[:, :, shift:], jnp.zeros((channels, seq_count, shift), running.dtype)], axis=2
        )
        running = running + factor * ahead
        factor = factor * factor
        shift *= 2
    return running.reshape(channels, -1)


def rate_term(adjoint, states_share, onehot, seq_count):
    channels = adjoint.shape[0]
    adjoint_seq = adjoint.reshape(channels, seq_count, -1)
    previous = states_share.astype(jnp.float32).reshape(channels, seq_count, -1)
    per_seq = jnp.sum(adjoint_seq[:, :, 1:] * previous[:, :, :-1], axis=2)
    return -jnp.dot(onehot.T, per_seq.T, precision=exact_mode)


def per_device(inputs, out_grad, states, in_weight, out_weight, decay_rate, session_ids, lengths):
    n_row = lax.axis_size("row")
    n_col = lax.axis_size("col")
    seq_count = session_ids.shape[0]
    onehot = session_table(session_ids, decay_rate.shape[0])
    grad_rows = gather_rows(out_grad, "col", n_col)
    token_total = grad_rows.shape[0]
    bin_count = token_total // seq_count
    token_ids = jnp.arange(token_total, dtype=jnp.int32)
    seq_match = (token_ids // bin_count)[:, None] == jnp.arange(seq_count, dtype=jnp.int32)[None, :]
    seq_length = jnp.sum(jnp.where(seq_match, lengths[None, :], 0), axis=1)
    valid_bin = token_ids % bin_count >= bin_count - seq_length
    masked = jnp.where(valid_bin[:, None], grad_rows, jnp.zeros_like(grad_rows))
    state_grad = scatter_sum(contract(out_weight, masked, 1, 1).astype(jnp.bfloat16), "row", n_row)
    states_rows = lax.all_gather(states, "row", axis=0, tiled=True)
    out_weight_grad = jnp.dot(states_rows, masked, preferred_element_type=jnp.float32).astype(
        jnp.bfloat16
    )
    adjoint = adjoint_sweep(state_grad, decay_rate, onehot, seq_count)
    rate_grad = rate_term(adjoint, states, onehot, seq_count)
    gathered = gather_rows(adjoint.astype(jnp.bfloat16), "row", n_row)
    input_rows = lax.all_gather(inputs, "col", axis=0, tiled=True)
    in_weight_grad = contract(input_rows, gathered, 0, 1).astype(jnp.bfloat16)
    input_grad = scatter_sum(
        contract(gathered, in_weight, 0, 1).astype(jnp.bfloat16), "col", n_col
    ).astype(jnp.bfloat16)
    return (input_grad, in_weight_grad, out_weight_grad, rate_grad)


def solution(mesh):
    return jax.shard_map(
        per_device,
        mesh=mesh,
        in_specs=(
            P("col", "row"),
            P("col", "row"),
            P(("col", "row"), None),
            P("row", "col"),
            P("col", "row"),
            P(None, ("col", "row")),
            P(),
            P(),
        ),
        out_specs=(P("col", "row"), P("row", "col"), P("col", "row"), P(None, ("col", "row"))),
        check_vma=False,
    )
```

profile of v0, /device:TPU:2, one launch (start us, length us, event | category | flops | bytes accessed | tf_op | source)
XLA Modules:
  0.0 284.3 jit_solution(6921144148416662720)
XLA Ops:
  7.2 0.0 copy-start
  7.2 2.6 broadcast_in_dim.26
  9.8 0.0 copy-start.3
  9.8 9.8 %all-to-all-start = ((bf16[16,64,1024]{2,1,0:T(8,128)(2,1)}), bf16[16,64,1024]{2,1,0:T(8,128)(2,1)}, u32[]{:S(2)}, u32[]{:S(2)}) async-start(bf16[16,64,1024]{2,1,0:T(8,128)(2,1)} %broadcast_in_dim.26), calls=%async_computation | async-start | bytes 4194304 | tf_op jit(solution)/shard_map/all_to_all | solution.py:26
  19.6 0.0 copy-done.3
  19.6 0.1 select_reduce_fusion
  19.7 50.4 %all-to-all-done = bf16[16,64,1024]{2,1,0:T(8,128)(2,1)} async-done(((bf16[16,64,1024]{2,1,0:T(8,128)(2,1)}), bf16[16,64,1024]{2,1,0:T(8,128)(2,1)}, u32[]{:S(2)}, u32[]{:S(2)}) %all-to-all-start) | async-done | bytes 2097184 | tf_op jit(solution)/shard_map/all_to_all | solution.py:26
  70.1 1.8 bitcast_select_fusion
  72.0 0.0 copy-done
  72.0 0.0 copy-start.1
  72.0 3.7 %convolution_convert_fusion.1 = bf16[1024,1024]{0,1:T(8,128)(2,1)} fusion(bf16[1024,1024]{1,0:T(8,128)(2,1)S(1)} %bitcast_select_fusion, bf16[1024,1024]{1,0:T(8,128)(2,1)S(1)} %copy-done), kind=kOutput, calls=%fused_computation.5 | convolution fusion | flops 2148532224 | bytes 6291456 | tf_op jit(solution)/shard_map/dot_general | solution.py:10
  75.7 0.0 copy-done.1
  75.7 0.0 copy-start.5
  75.7 7.3 %all-to-all-start.1 = ((bf16[16,64,1024]{2,1,0:T(8,128)(2,1)}), bf16[16,64,1024]{2,1,0:T(8,128)(2,1)}, u32[]{:S(2)}, u32[]{:S(2)}) async-start(bf16[16,64,1024]{2,1,0:T(8,128)(2,1)} %bitcast.25), calls=%async_computation.1 | async-start | bytes 4194304 | tf_op jit(solution)/shard_map/all_to_all | solution.py:30
  83.0 0.0 all-gather.5.cloned.1.call-start
  83.1 0.7 all-gather.5.cloned.1.call-update
  83.7 0.0 copy-done.4
  83.8 0.0 copy-done.5
  83.8 0.2 multiply_multiply_fusion
  84.0 0.1 copy.22
  84.1 0.1 copy.23
  84.1 0.1 copy.24
  84.2 0.1 copy.25
  84.3 0.1 copy.26
  84.4 0.1 copy.27
  84.5 0.1 copy.28
  84.6 0.1 copy.29
  84.7 28.2 %all-to-all-done.1 = bf16[16,64,1024]{2,1,0:T(8,128)(2,1)} async-done(((bf16[16,64,1024]{2,1,0:T(8,128)(2,1)}), bf16[16,64,1024]{2,1,0:T(8,128)(2,1)}, u32[]{:S(2)}, u32[]{:S(2)}) %all-to-all-start.1) | async-done | bytes 2097184 | tf_op jit(solution)/shard_map/all_to_all | solution.py:30
  112.9 2.0 convert_reduce_fusion
  114.9 0.1 reshape.80
  115.0 0.2 slice.44
  115.2 0.2 multiply_add_fusion.7
  115.4 0.2 slice.45
  115.6 0.1 multiply_add_fusion.6
  115.7 0.2 slice.46
  115.9 0.1 multiply_add_fusion.5
  116.1 0.2 slice.47
  116.3 0.1 multiply_add_fusion.4
  116.4 0.2 slice.48
  116.6 0.1 multiply_add_fusion.3
  116.8 0.2 slice.49
  117.0 0.1 multiply_add_fusion.2
  117.1 0.2 slice.50
  117.3 0.1 multiply_add_fusion.1
  117.5 0.1 fusion.14
  117.7 1.6 broadcast_in_dim.28
  119.3 5.7 %all-to-all-start.2 = ((bf16[16,64,1024]{2,1,0:T(8,128)(2,1)}), bf16[16,64,1024]{2,1,0:T(8,128)(2,1)}, u32[]{:S(2)}, u32[]{:S(2)}) async-start(bf16[16,64,1024]{2,1,0:T(8,128)(2,1)} %broadcast_in_dim.28), calls=%async_computation.2 | async-start | bytes 4194304 | tf_op jit(solution)/shard_map/all_to_all | solution.py:26
  125.0 0.0 all-gather.3.cloned.1.call-start
  125.0 0.7 all-gather.3.cloned.1.call-update
  125.7 30.0 %all-to-all-done.2 = bf16[16,64,1024]{2,1,0:T(8,128)(2,1)} async-done(((bf16[16,64,1024]{2,1,0:T(8,128)(2,1)}), bf16[16,64,1024]{2,1,0:T(8,128)(2,1)}, u32[]{:S(2)}, u32[]{:S(2)}) %all-to-all-start.2) | async-done | bytes 2097184 | tf_op jit(solution)/shard_map/all_to_all | solution.py:26
  155.7 5.9 %convolution_convert_fusion = bf16[1024,1024]{1,0:T(8,128)(2,1)} fusion(bf16[1024,1024]{1,0:T(8,128)(2,1)} %bitcast.4, bf16[1024,1024]{1,0:T(8,128)(2,1)} %param.11), kind=kOutput, calls=%fused_computation.4 | convolution fusion | flops 2148532224 | bytes 6291456 | tf_op jit(solution)/shard_map/dot_general | solution.py:10
  161.7 4.7 %all-to-all-start.3 = ((bf16[16,64,1024]{2,1,0:T(8,128)(2,1)}), bf16[16,64,1024]{2,1,0:T(8,128)(2,1)}, u32[]{:S(2)}, u32[]{:S(2)}) async-start(bf16[16,64,1024]{2,1,0:T(8,128)(2,1)} %bitcast.26), calls=%async_computation.3 | async-start | bytes 4194304 | tf_op jit(solution)/shard_map/all_to_all | solution.py:30
  166.4 0.0 copy-done.2
  166.4 0.1 reshape.83
  166.5 0.0 all-gather.5.cloned.1.call-done
  166.5 5.9 %convert_bitcast_fusion = bf16[1024,1024]{0,1:T(8,128)(2,1)} fusion(bf16[1024,1024]{1,0:T(8,128)(2,1)} %copy-done.1, bf16[1024,1024]{1,0:T(8,128)(2,1)} %all-gather.5.cloned.1.call-done), kind=kOutput, calls=%fused_computation.2 | convolution fusion | flops 2148532224 | bytes 6291456 | tf_op jit(solution)/shard_map/dot_general | solution.py:75
  172.5 3.9 %copy.31 = bf16[1024,1024]{1,0:T(8,128)(2,1)} copy(bf16[1024,1024]{0,1:T(8,128)(2,1)} %convert_bitcast_fusion) | data formatting | bytes 4194304
  176.4 0.3 fusion.1
  176.7 0.9 convolution_negate_fusion
  177.6 87.4 %all-gather.3.cloned.1.call-done = bf16[1024,1024]{1,0:T(8,128)(2,1)} async-done(((bf16[64,1024]{1,0:T(8,128)(2,1)}), bf16[1024,1024]{1,0:T(8,128)(2,1)}) %all-gather.3.cloned.1.call-update) | async-done | bytes 2097168 | tf_op jit(solution)/shard_map/all_gather | solution.py:81
  265.0 5.9 %convert_bitcast_fusion.1 = bf16[1024,1024]{0,1:T(8,128)(2,1)} fusion(bf16[1024,1024]{1,0:T(8,128)(2,1)} %bitcast.4, bf16[1024,1024]{1,0:T(8,128)(2,1)} %all-gather.3.cloned.1.call-done), kind=kOutput, calls=%fused_computation.3 | convolution fusion | flops 2148532224 | bytes 6291456 | tf_op jit(solution)/shard_map/dot_general | solution.py:10
  270.9 3.9 %copy.30 = bf16[1024,1024]{1,0:T(8,128)(2,1)} copy(bf16[1024,1024]{0,1:T(8,128)(2,1)} %convert_bitcast_fusion.1) | data formatting | bytes 4194304
  274.8 0.0 all-to-all-done.3
  274.8 2.7 reduce_sum.41
  (6 shorter events, 0.1 us)
Async XLA Ops:
  7.2 64.8 %copy-start = (bf16[1024,1024]{1,0:T(8,128)(2,1)S(1)}, bf16[1024,1024]{1,0:T(8,128)(2,1)}, u32[]{:S(2)}) copy-start(bf16[1024,1024]{1,0:T(8,128)(2,1)} %param.12) | copy-start | bytes 6291460
  9.8 9.8 %copy-start.3 = (s32[4]{0:T(128)S(1)}, s32[4]{0:T(128)}, u32[]{:S(2)}) copy-start(s32[4]{0:T(128)} %param.15) | copy-start | bytes 52
  9.8 60.3 %all-to-all-start = ((bf16[16,64,1024]{2,1,0:T(8,128)(2,1)}), bf16[16,64,1024]{2,1,0:T(8,128)(2,1)}, u32[]{:S(2)}, u32[]{:S(2)}) async-start(bf16[16,64,1024]{2,1,0:T(8,128)(2,1)} %broadcast_in_dim.26), calls=%async_computation | async-start | bytes 4194304 | tf_op jit(solution)/shard_map/all_to_all | solution.py:26
  72.0 3.7 %copy-start.1 = (bf16[1024,1024]{1,0:T(8,128)(2,1)}, bf16[1024,1024]{1,0:T(8,128)(2,1)S(1)}, u32[]{:S(2)}) copy-start(bf16[1024,1024]{1,0:T(8,128)(2,1)S(1)} %bitcast_select_fusion) | copy-start | bytes 6291460
  75.7 8.1 %copy-start.4 = (f32[4,64]{1,0:T(4,128)S(1)}, f32[4,64]{1,0:T(4,128)}, u32[]{:S(2)}) copy-start(f32[4,64]{1,0:T(4,128)} %param.13) | copy-start | bytes 3076
  75.7 8.1 %copy-start.5 = (s32[4]{0:T(128)S(1)}, s32[4]{0:T(128)}, u32[]{:S(2)}) copy-start(s32[4]{0:T(128)} %param.14) | copy-start | bytes 52
  75.7 37.2 %all-to-all-start.1 = ((bf16[16,64,1024]{2,1,0:T(8,128)(2,1)}), bf16[16,64,1024]{2,1,0:T(8,128)(2,1)}, u32[]{:S(2)}, u32[]{:S(2)}) async-start(bf16[16,64,1024]{2,1,0:T(8,128)(2,1)} %bitcast.25), calls=%async_computation.1 | async-start | bytes 4194304 | tf_op jit(solution)/shard_map/all_to_all | solution.py:30
  83.0 83.5 %all-gather.5.cloned.1.call-start = ((), (), s32[]{:S(2)}) async-start(), calls=%async_computation.5 | async-start | bytes 2228224 | tf_op jit(solution)/shard_map/all_gather | solution.py:74
  119.3 36.5 %all-to-all-start.2 = ((bf16[16,64,1024]{2,1,0:T(8,128)(2,1)}), bf16[16,64,1024]{2,1,0:T(8,128)(2,1)}, u32[]{:S(2)}, u32[]{:S(2)}) async-start(bf16[16,64,1024]{2,1,0:T(8,128)(2,1)} %broadcast_in_dim.28), calls=%async_computation.2 | async-start | bytes 4194304 | tf_op jit(solution)/shard_map/all_to_all | solution.py:26
  125.0 140.0 %all-gather.3.cloned.1.call-start = ((), (), s32[]{:S(2)}) async-start(), calls=%async_computation.4 | async-start | bytes 2228224 | tf_op jit(solution)/shard_map/all_gather | solution.py:81
  161.7 4.8 %copy-start.2 = (bf16[64,1024]{1,0:T(8,128)(2,1)S(1)}, bf16[64,1024]{1,0:T(8,128)(2,1)}, u32[]{:S(2)}) copy-start(bf16[64,1024]{1,0:T(8,128)(2,1)} %param.10) | copy-start | bytes 393220
  161.7 113.1 %all-to-all-start.3 = ((bf16[16,64,1024]{2,1,0:T(8,128)(2,1)}), bf16[16,64,1024]{2,1,0:T(8,128)(2,1)}, u32[]{:S(2)}, u32[]{:S(2)}) async-start(bf16[16,64,1024]{2,1,0:T(8,128)(2,1)} %bitcast.26), calls=%async_computation.3 | async-start | bytes 4194304 | tf_op jit(solution)/shard_map/all_to_all | solution.py:30
Sparse Core Ops, SparseCore 0:
  86.5 76.7 all-gather.4
  165.2 99.7 all-gather.2
where the time goes:
time: 285 us; the launch traced here: 284 us
  waiting for transfers between devices  197 us (69%)
  starting transfers between devices  27.6 us (10%)
  matrix products  22.5 us (8%)
  local copies, waits for them, and re-layouts  14.5 us (5%)
  between operations  14.3 us (5%)
  other arithmetic  8.02 us (3%)
    all_gather x1, waiting for transfers between devices, per_device(): input_rows = lax.all_gather(inputs, 'col', axis=0, tiled=True)  87.4 us
    all_to_all x2, waiting for transfers between devices, gather_rows(): lax.all_to_all(spread, axis_name, 0, 0).reshape((-1,) + share.shape[1:])  80.5 us
    all_to_all x2, waiting for transfers between devices, scatter_sum(): lax.all_to_all(partial.reshape((parts, -1) + partial.shape[1:]), axis_nam...  28.2 us
    dot_general x3, matrix products, contract(): lax.dot_general(left_side, right_side, (((left_dim,), (right_dim,)), ((),...  15.5 us
    all_to_all x2, starting transfers between devices, gather_rows(): lax.all_to_all(spread, axis_name, 0, 0).reshape((-1,) + share.shape[1:])  15.5 us
    all_to_all x2, starting transfers between devices, scatter_sum(): lax.all_to_all(partial.reshape((parts, -1) + partial.shape[1:]), axis_nam...  12.1 us
    unnamed x15, local copies, waits for them, and re-layouts  7.91 us
    dot_general x1, matrix products, per_device(): jnp.dot(states_rows, masked, preferred_element_type=jnp.float32)  5.94 us
  transfers between devices with their start and end apart: 6, of which 4 were waited for; matrix products, arithmetic and copies ran while one was open for 12% of the time, Pallas kernels for 0%

commit v1 on v0

--- a/solution.py
+++ b/solution.py
@@ -78,7 +78,14 @@
     adjoint = adjoint_sweep(state_grad, decay_rate, onehot, seq_count)
     rate_grad = rate_term(adjoint, states, onehot, seq_count)
     gathered = gather_rows(adjoint.astype(jnp.bfloat16), "row", n_row)
-    input_rows = lax.all_gather(inputs, "col", axis=0, tiled=True)
+
+    def set_sizes(raw):
+        near = jax.lax.axis_size("col")
+        a_now = jnp.stack([raw] * near)
+        y = jax.lax.all_to_all(a_now, "col", split_axis=0, concat_axis=0)
+        return jnp.concatenate(y, axis=0)
+
+    input_rows = set_sizes(inputs)
     in_weight_grad = contract(input_rows, gathered, 0, 1).astype(jnp.bfloat16)
     input_grad = scatter_sum(
         contract(gathered, in_weight, 0, 1).astype(jnp.bfloat16), "col", n_col

time: 285 us -> 273 us (0.958)
  waiting for transfers between devices: 197 us -> 154 us
  blocking collectives: 0 us -> 30.8 us
    all_gather x1 -> x0, waiting for transfers between devices: 87.4 us -> none  [per_device(): input_rows = lax.all_gather(inputs, 'col', axis=0, tiled=True)]
    all_to_all x0 -> x1, waiting for transfers between devices: none -> 45.7 us  [set_sizes(): y = jax.lax.all_to_all(a_now, 'col', split_axis=0, concat_axis=0)]
    all_to_all x0 -> x1, blocking collectives: none -> 30.8 us  [gather_rows(): lax.all_to_all(spread, axis_name, 0, 0).reshape((-1,) + share.shape[1:])]
    all_to_all x2 -> x1, waiting for transfers between devices: 80.5 us -> 50.4 us  [gather_rows(): lax.all_to_all(spread, axis_name, 0, 0).reshape((-1,) + share.shape[1:])]
    all_to_all x2, waiting for transfers between devices: 28.2 us -> 50.4 us  [scatter_sum(): lax.all_to_all(partial.reshape((parts, -1) + partial.shape[1:]), axis_nam...]
    all_gather x1, waiting for transfers between devices: 0.02 us -> 6.9 us  [per_device(): states_rows = lax.all_gather(states, 'row', axis=0, tiled=True)]
    all_to_all x2 -> x1, starting transfers between devices: 15.5 us -> 9.76 us  [gather_rows(): lax.all_to_all(spread, axis_name, 0, 0).reshape((-1,) + share.shape[1:])]
    all_to_all x0 -> x1, starting transfers between devices: none -> 4.44 us  [set_sizes(): y = jax.lax.all_to_all(a_now, 'col', split_axis=0, concat_axis=0)]
  transfers between devices with their start and end apart: 6 -> 5, of which waited for: 4 -> 5; matrix products, arithmetic and copies ran while one was open for 12% -> 10% of each run, Pallas kernels for 0% -> 0%
where the time goes in v1:
time: 273 us; the launch traced here: 272 us
  waiting for transfers between devices  154 us (56%)
  blocking collectives  30.8 us (11%)
  starting transfers between devices  27.3 us (10%)
  matrix products  22.6 us (8%)
  local copies, waits for them, and re-layouts  14.7 us (5%)
  between operations  14.3 us (5%)
  other arithmetic  8.02 us (3%)
    all_to_all x1, waiting for transfers between devices, gather_rows(): lax.all_to_all(spread, axis_name, 0, 0).reshape((-1,) + share.shape[1:])  50.4 us
    all_to_all x2, waiting for transfers between devices, scatter_sum(): lax.all_to_all(partial.reshape((parts, -1) + partial.shape[1:]), axis_nam...  50.4 us
    all_to_all x1, waiting for transfers between devices, set_sizes(): y = jax.lax.all_to_all(a_now, 'col', split_axis=0, concat_axis=0)  45.7 us
    all_to_all x1, blocking collectives, gather_rows(): lax.all_to_all(spread, axis_name, 0, 0).reshape((-1,) + share.shape[1:])  30.8 us
    dot_general x3, matrix products, contract(): lax.dot_general(left_side, right_side, (((left_dim,), (right_dim,)), ((),...  15.6 us
    all_to_all x2, starting transfers between devices, scatter_sum(): lax.all_to_all(partial.reshape((parts, -1) + partial.shape[1:]), axis_nam...  13.1 us
    all_to_all x1, starting transfers between devices, gather_rows(): lax.all_to_all(spread, axis_name, 0, 0).reshape((-1,) + share.shape[1:])  9.76 us
    unnamed x17, local copies, waits for them, and re-layouts  7.92 us
  transfers between devices with their start and end apart: 5, of which 5 were waited for; matrix products, arithmetic and copies ran while one was open for 10% of the time, Pallas kernels for 0%

profile of v1, /device:TPU:2, one launch (start us, length us, event | category | flops | bytes accessed | tf_op | source)
XLA Modules:
  0.0 271.8 jit_solution(16994372228694212993)
XLA Ops:
  7.2 0.0 copy-start
  7.2 2.6 broadcast_in_dim.26
  9.8 0.0 copy-start.4
  9.8 9.8 %all-to-all-start = ((bf16[16,64,1024]{2,1,0:T(8,128)(2,1)}), bf16[16,64,1024]{2,1,0:T(8,128)(2,1)}, u32[]{:S(2)}, u32[]{:S(2)}) async-start(bf16[16,64,1024]{2,1,0:T(8,128)(2,1)} %broadcast_in_dim.26), calls=%async_computation | async-start | bytes 4194304 | tf_op jit(solution)/shard_map/all_to_all | solution.py:26
  19.6 0.0 copy-done.4
  19.6 0.1 select_reduce_fusion
  19.7 50.4 %all-to-all-done = bf16[16,64,1024]{2,1,0:T(8,128)(2,1)} async-done(((bf16[16,64,1024]{2,1,0:T(8,128)(2,1)}), bf16[16,64,1024]{2,1,0:T(8,128)(2,1)}, u32[]{:S(2)}, u32[]{:S(2)}) %all-to-all-start) | async-done | bytes 2097184 | tf_op jit(solution)/shard_map/all_to_all | solution.py:26
  70.1 1.8 bitcast_select_fusion
  72.0 0.0 copy-done
  72.0 0.0 copy-start.1
  72.0 3.7 %convolution_convert_fusion.1 = bf16[1024,1024]{0,1:T(8,128)(2,1)} fusion(bf16[1024,1024]{1,0:T(8,128)(2,1)S(1)} %bitcast_select_fusion, bf16[1024,1024]{1,0:T(8,128)(2,1)S(1)} %copy-done), kind=kOutput, calls=%fused_computation.5 | convolution fusion | flops 2148532224 | bytes 6291456 | tf_op jit(solution)/shard_map/dot_general | solution.py:10
  75.7 0.0 copy-done.1
  75.7 7.3 %all-to-all-start.1 = ((bf16[16,64,1024]{2,1,0:T(8,128)(2,1)}), bf16[16,64,1024]{2,1,0:T(8,128)(2,1)}, u32[]{:S(2)}, u32[]{:S(2)}) async-start(bf16[16,64,1024]{2,1,0:T(8,128)(2,1)} %bitcast.28), calls=%async_computation.1 | async-start | bytes 4194304 | tf_op jit(solution)/shard_map/all_to_all | solution.py:30
  83.0 0.0 copy-done.5
  83.0 0.0 copy-done.6
  83.0 0.2 multiply_multiply_fusion
  83.2 0.1 copy.22
  83.3 0.1 copy.23
  83.4 0.1 copy.24
  83.5 0.1 copy.25
  83.6 0.1 copy.26
  83.7 0.1 copy.27
  83.8 0.1 copy.28
  83.9 0.1 copy.29
  84.0 27.7 %all-to-all-done.1 = bf16[16,64,1024]{2,1,0:T(8,128)(2,1)} async-done(((bf16[16,64,1024]{2,1,0:T(8,128)(2,1)}), bf16[16,64,1024]{2,1,0:T(8,128)(2,1)}, u32[]{:S(2)}, u32[]{:S(2)}) %all-to-all-start.1) | async-done | bytes 2097184 | tf_op jit(solution)/shard_map/all_to_all | solution.py:30
  111.7 2.0 convert_reduce_fusion
  113.7 0.1 reshape.85
  113.8 0.2 slice.44
  114.0 0.1 multiply_add_fusion.7
  114.2 0.2 slice.45
  114.3 0.1 multiply_add_fusion.6
  114.5 0.2 slice.46
  114.7 0.1 multiply_add_fusion.5
  114.8 0.2 slice.47
  115.0 0.1 multiply_add_fusion.4
  115.2 0.2 slice.48
  115.4 0.1 multiply_add_fusion.3
  115.5 0.2 slice.49
  115.7 0.1 multiply_add_fusion.2
  115.9 0.2 slice.50
  116.1 0.1 multiply_add_fusion.1
  116.3 0.1 fusion.14
  116.5 0.3 broadcast_in_dim.28
  116.7 0.0 copy-start.3
  116.7 30.8 %all_to_all.25 = bf16[16,64,1024]{2,1,0:T(8,128)(2,1)} all-to-all(bf16[16,64,1024]{2,1,0:T(8,128)(2,1)S(1)} %broadcast_in_dim.28), channel_id=1, replica_groups=mesh['row'=16,'col'=16] {'row'}, dimensions={0} | all-to-all | bytes 4194304 | tf_op jit(solution)/shard_map/all_to_all | solution.py:26
  147.5 0.0 copy-done.3
  147.5 1.6 stack.2
  149.1 4.4 %all-to-all-start.4 = ((bf16[16,64,1024]{2,1,0:T(8,128)(2,1)}), bf16[16,64,1024]{2,1,0:T(8,128)(2,1)}, u32[]{:S(2)}, u32[]{:S(2)}) async-start(bf16[16,64,1024]{2,1,0:T(8,128)(2,1)} %stack.2), calls=%async_computation.4 | async-start | bytes 4194304 | tf_op jit(solution)/shard_map/all_to_all | solution.py:85
  153.5 0.0 all-gather.2.cloned.1.call-start
  153.6 0.7 all-gather.2.cloned.1.call-update
  154.3 6.0 %convolution_convert_fusion = bf16[1024,1024]{1,0:T(8,128)(2,1)} fusion(bf16[1024,1024]{1,0:T(8,128)(2,1)} %bitcast.26, bf16[1024,1024]{1,0:T(8,128)(2,1)} %param.11), kind=kOutput, calls=%fused_computation.4 | convolution fusion | flops 2148532224 | bytes 6291456 | tf_op jit(solution)/shard_map/dot_general | solution.py:10
  160.2 45.7 %all-to-all-done.4 = bf16[16,64,1024]{2,1,0:T(8,128)(2,1)} async-done(((bf16[16,64,1024]{2,1,0:T(8,128)(2,1)}), bf16[16,64,1024]{2,1,0:T(8,128)(2,1)}, u32[]{:S(2)}, u32[]{:S(2)}) %all-to-all-start.4) | async-done | bytes 2097184 | tf_op jit(solution)/shard_map/all_to_all | solution.py:85
  205.9 5.8 %all-to-all-start.3 = ((bf16[16,64,1024]{2,1,0:T(8,128)(2,1)}), bf16[16,64,1024]{2,1,0:T(8,128)(2,1)}, u32[]{:S(2)}, u32[]{:S(2)}) async-start(bf16[16,64,1024]{2,1,0:T(8,128)(2,1)} %bitcast.29), calls=%async_computation.3 | async-start | bytes 4194304 | tf_op jit(solution)/shard_map/all_to_all | solution.py:30
  211.7 0.0 copy-done.2
  211.7 0.1 reshape.89
  211.8 6.9 %all-gather.2.cloned.1.call-done = bf16[1024,1024]{1,0:T(8,128)(2,1)} async-done(((bf16[64,1024]{1,0:T(8,128)(2,1)}), bf16[1024,1024]{1,0:T(8,128)(2,1)}) %all-gather.2.cloned.1.call-update) | async-done | bytes 2097168 | tf_op jit(solution)/shard_map/all_gather | solution.py:74
  218.7 5.9 %convert_bitcast_fusion = bf16[1024,1024]{0,1:T(8,128)(2,1)} fusion(bf16[1024,1024]{1,0:T(8,128)(2,1)} %copy-done.1, bf16[1024,1024]{1,0:T(8,128)(2,1)} %all-gather.2.cloned.1.call-done), kind=kOutput, calls=%fused_computation.2 | convolution fusion | flops 2148532224 | bytes 6291456 | tf_op jit(solution)/shard_map/dot_general | solution.py:75
  224.6 3.9 %copy.31 = bf16[1024,1024]{1,0:T(8,128)(2,1)} copy(bf16[1024,1024]{0,1:T(8,128)(2,1)} %convert_bitcast_fusion) | data formatting | bytes 4194304
  228.6 0.3 fusion.1
  228.9 0.9 convolution_negate_fusion
  229.7 5.9 %convert_bitcast_fusion.1 = bf16[1024,1024]{0,1:T(8,128)(2,1)} fusion(bf16[1024,1024]{1,0:T(8,128)(2,1)} %bitcast.27, bf16[1024,1024]{1,0:T(8,128)(2,1)} %bitcast.6), kind=kOutput, calls=%fused_computation.3 | convolution fusion | flops 2148532224 | bytes 6291456 | tf_op jit(solution)/shard_map/dot_general | solution.py:10
  235.7 3.9 %copy.30 = bf16[1024,1024]{1,0:T(8,128)(2,1)} copy(bf16[1024,1024]{0,1:T(8,128)(2,1)} %convert_bitcast_fusion.1) | data formatting | bytes 4194304
  239.6 22.7 %all-to-all-done.3 = bf16[16,64,1024]{2,1,0:T(8,128)(2,1)} async-done(((bf16[16,64,1024]{2,1,0:T(8,128)(2,1)}), bf16[16,64,1024]{2,1,0:T(8,128)(2,1)}, u32[]{:S(2)}, u32[]{:S(2)}) %all-to-all-start.3) | async-done | bytes 2097184 | tf_op jit(solution)/shard_map/all_to_all | solution.py:30
  262.3 2.7 reduce_sum.41
  (7 shorter events, 0.1 us)
Async XLA Ops:
  7.2 64.8 %copy-start = (bf16[1024,1024]{1,0:T(8,128)(2,1)S(1)}, bf16[1024,1024]{1,0:T(8,128)(2,1)}, u32[]{:S(2)}) copy-start(bf16[1024,1024]{1,0:T(8,128)(2,1)} %param.12) | copy-start | bytes 6291460
  9.8 9.8 %copy-start.4 = (s32[4]{0:T(128)S(1)}, s32[4]{0:T(128)}, u32[]{:S(2)}) copy-start(s32[4]{0:T(128)} %param.15) | copy-start | bytes 52
  9.8 60.3 %all-to-all-start = ((bf16[16,64,1024]{2,1,0:T(8,128)(2,1)}), bf16[16,64,1024]{2,1,0:T(8,128)(2,1)}, u32[]{:S(2)}, u32[]{:S(2)}) async-start(bf16[16,64,1024]{2,1,0:T(8,128)(2,1)} %broadcast_in_dim.26), calls=%async_computation | async-start | bytes 4194304 | tf_op jit(solution)/shard_map/all_to_all | solution.py:26
  72.0 3.7 %copy-start.1 = (bf16[1024,1024]{1,0:T(8,128)(2,1)}, bf16[1024,1024]{1,0:T(8,128)(2,1)S(1)}, u32[]{:S(2)}) copy-start(bf16[1024,1024]{1,0:T(8,128)(2,1)S(1)} %bitcast_select_fusion) | copy-start | bytes 6291460
  75.7 7.3 %copy-start.5 = (f32[4,64]{1,0:T(4,128)S(1)}, f32[4,64]{1,0:T(4,128)}, u32[]{:S(2)}) copy-start(f32[4,64]{1,0:T(4,128)} %param.13) | copy-start | bytes 3076
  75.7 7.3 %copy-start.6 = (s32[4]{0:T(128)S(1)}, s32[4]{0:T(128)}, u32[]{:S(2)}) copy-start(s32[4]{0:T(128)} %param.14) | copy-start | bytes 52
  75.7 36.0 %all-to-all-start.1 = ((bf16[16,64,1024]{2,1,0:T(8,128)(2,1)}), bf16[16,64,1024]{2,1,0:T(8,128)(2,1)}, u32[]{:S(2)}, u32[]{:S(2)}) async-start(bf16[16,64,1024]{2,1,0:T(8,128)(2,1)} %bitcast.28), calls=%async_computation.1 | async-start | bytes 4194304 | tf_op jit(solution)/shard_map/all_to_all | solution.py:30
  116.7 30.8 %copy-start.3 = (bf16[64,1024]{1,0:T(8,128)(2,1)S(1)}, bf16[64,1024]{1,0:T(8,128)(2,1)}, u32[]{:S(2)}) copy-start(bf16[64,1024]{1,0:T(8,128)(2,1)} %param.8) | copy-start | bytes 393220
  149.1 56.9 %all-to-all-start.4 = ((bf16[16,64,1024]{2,1,0:T(8,128)(2,1)}), bf16[16,64,1024]{2,1,0:T(8,128)(2,1)}, u32[]{:S(2)}, u32[]{:S(2)}) async-start(bf16[16,64,1024]{2,1,0:T(8,128)(2,1)} %stack.2), calls=%async_computation.4 | async-start | bytes 4194304 | tf_op jit(solution)/shard_map/all_to_all | solution.py:85
  153.5 65.2 %all-gather.2.cloned.1.call-start = ((), (), s32[]{:S(2)}) async-start(), calls=%async_computation.5 | async-start | bytes 2228224 | tf_op jit(solution)/shard_map/all_gather | solution.py:74
  205.9 5.8 %copy-start.2 = (bf16[64,1024]{1,0:T(8,128)(2,1)S(1)}, bf16[64,1024]{1,0:T(8,128)(2,1)}, u32[]{:S(2)}) copy-start(bf16[64,1024]{1,0:T(8,128)(2,1)} %param.10) | copy-start | bytes 393220
  205.9 56.3 %all-to-all-start.3 = ((bf16[16,64,1024]{2,1,0:T(8,128)(2,1)}), bf16[16,64,1024]{2,1,0:T(8,128)(2,1)}, u32[]{:S(2)}, u32[]{:S(2)}) async-start(bf16[16,64,1024]{2,1,0:T(8,128)(2,1)} %bitcast.29), calls=%async_computation.3 | async-start | bytes 4194304 | tf_op jit(solution)/shard_map/all_to_all | solution.py:30
Sparse Core Ops, SparseCore 0:
  157.1 61.6 all-gather.1
